TPU v7x, 256 devices: a whole 4x4x8 slice. The times are simulated.
256 devices in a mesh: wide: 16 (over z, core), narrow: 16 (over y, x).
Axes of the slice: x: 4, y: 4, z: 8, core: 2. Of those that a mesh axis runs over, the one named last changes fastest.
Arguments:
- screens: bfloat16 [4, 4096, 4096], P(None, 'wide'), may hold values from -3 to 3
- offsets: int32 [2, 128, 4], replicated, may hold values from 0 to 2752, as said below
- valid: int32 [2, 80, 80], P(None, 'narrow'), may hold values from 0 to 1, as said below
- recon: bfloat16 [25600, 5120], P('narrow', 'wide'), may hold values from -0.0390625 to 0.0390625
Outputs:
- slopes: float32 [2, 64, 2, 80, 80], P(None, 'wide', None, 'narrow')
- commands: float32 [64, 5120], P('narrow', 'wide')
Inputs may be any that keep to these rules, and one draw needn't show every extreme that they name: For each coordinate and each layer, the offsets of all items lie within 64 of the smallest, and the largest is exactly 64 above the smallest. In the 5 subaperture rows of one index of narrow, each sensor has at most 300 valid subapertures; in every draw one index of narrow holds exactly 300 for each sensor.
All inputs are finite; a program needn't handle non-finite values.
Results may differ from a plain program's by a relative error of at most 0.0043.
Values may be sent and summed in bfloat16 or wider, within the bound.
No kernel may reach another device: no remote copies, remote signals or barrier semaphores. Data moves between devices by JAX's collectives and lax.ppermute only.
A program may use at most 128 MiB of HBM per device.

v0:
```python
import math
import jax
import jax.numpy as jnp
from jax import lax
from jax.sharding import PartitionSpec as P

L = 4
NSUB = 80
SAMP = 16
NPIX = 32
NSENS = 2
SPREAD = 64
FR_DEV = 4
PUP = 1280


def broadcast(block, axis, source):
    block = jnp.where(lax.axis_index(axis) == source, block, jnp.zeros_like(block))
    return lax.psum(block, axis)


def dft_table(samp, npix):
    sample_ids = jnp.arange(samp * samp, dtype=jnp.int32)
    pixel_ids = jnp.arange(npix * npix, dtype=jnp.int32)
    sample_row = sample_ids // samp
    sample_col = sample_ids % samp
    pixel_row = pixel_ids // npix - npix // 2
    pixel_col = pixel_ids % npix - npix // 2
    phase_turns = jnp.mod(
        sample_row[:, None] * pixel_row[None, :] + sample_col[:, None] * pixel_col[None, :], npix
    )
    angles = phase_turns.astype(jnp.float32) * jnp.float32(-2.0 * math.pi / npix)
    cosine = jnp.cos(angles).astype(jnp.bfloat16)
    sine_part = jnp.sin(angles).astype(jnp.bfloat16)
    top_rows = jnp.concatenate([cosine, sine_part], axis=1)
    bottom_rows = jnp.concatenate([-sine_part, cosine], axis=1)
    return jnp.concatenate([top_rows, bottom_rows], axis=0)


def subaperture_fields(pupil_phase, samp):
    sub_rows = pupil_phase.shape[0] // samp
    sub_cols = pupil_phase.shape[1] // samp
    samples = (
        pupil_phase.reshape(sub_rows, samp, sub_cols, samp)
        .transpose(0, 2, 1, 3)
        .reshape(sub_rows * sub_cols, samp * samp)
    )
    return jnp.concatenate([jnp.cos(samples), jnp.sin(samples)], axis=1).astype(jnp.bfloat16)


def centroids(fields, transform, npix):
    spectrum = jnp.dot(fields, transform, preferred_element_type=jnp.float32)
    pixel_count = npix * npix
    real_part = spectrum[:, :pixel_count]
    imag_part = spectrum[:, pixel_count:]
    intensity = real_part * real_part + imag_part * imag_part
    pixel_ids = jnp.arange(pixel_count, dtype=jnp.int32)
    along_x = (pixel_ids % npix - npix // 2).astype(jnp.float32)
    along_y = (pixel_ids // npix - npix // 2).astype(jnp.float32)
    flux_total = jnp.sum(intensity, axis=1)
    centre_x = jnp.sum(intensity * along_x[None, :], axis=1) / flux_total
    centre_y = jnp.sum(intensity * along_y[None, :], axis=1) / flux_total
    return jnp.stack([centre_x, centre_y], axis=1)


def body(screens, offsets, valid, recon):
    narrow_count = lax.axis_size("narrow")
    wide_index = lax.axis_index("wide")
    narrow_index = lax.axis_index("narrow")
    band_rows = screens.shape[1]
    sub_rows = valid.shape[1]
    pixel_rows = sub_rows * SAMP
    slab_rows = pixel_rows + SPREAD
    union_cols = PUP + SPREAD
    local_items = FR_DEV * NSENS
    own_offsets = lax.dynamic_slice_in_dim(offsets, wide_index * local_items, local_items, 1)
    lowest = jnp.min(offsets, axis=1)
    pad = jnp.zeros((slab_rows, union_cols), screens.dtype)
    slabs = []
    for which_layer in range(L):
        band = lax.dynamic_slice_in_dim(screens[which_layer], lowest[1, which_layer], union_cols, 1)
        padded = jnp.concatenate([pad, band, pad], axis=0)
        group_start = lowest[0, which_layer] + pixel_rows * narrow_index
        row_at = jnp.clip(
            group_start - wide_index * band_rows + slab_rows, 0, band_rows + slab_rows
        )
        slabs.append(lax.dynamic_slice_in_dim(padded, row_at, slab_rows, 0))
    slabs = lax.psum(jnp.stack(slabs), "wide")
    rel = own_offsets - lowest[:, None, :]
    phases = []
    for item in range(local_items):
        acc = jnp.zeros((pixel_rows, PUP), jnp.float32)
        for which_layer in range(L):
            window = lax.dynamic_slice(
                slabs[which_layer],
                (rel[0, item, which_layer], rel[1, item, which_layer]),
                (pixel_rows, PUP),
            )
            acc = acc + window.astype(jnp.float32)
        phases.append(acc)
    pupil_phase = jnp.stack(phases)
    transform = dft_table(SAMP, NPIX)
    frame_phase = pupil_phase.reshape(FR_DEV, NSENS, pixel_rows, PUP)
    valid_flags = valid.reshape(-1)

    def frame_fields(frame_block):
        return jnp.concatenate(
            [subaperture_fields(frame_block[sensor_index], SAMP) for sensor_index in range(NSENS)],
            axis=0,
        )

    def one_frame(frame_block):
        return centroids(frame_fields(frame_block), transform, NPIX) * valid_flags[:, None].astype(
            jnp.float32
        )

    measured = lax.map(one_frame, frame_phase)
    measured = measured.reshape(FR_DEV, NSENS, sub_rows, NSUB, 2)
    slopes = measured.transpose(4, 0, 1, 2, 3)
    slope_vector = (
        measured.transpose(0, 2, 1, 3, 4)
        .reshape(FR_DEV, sub_rows * NSENS * NSUB * 2)
        .astype(jnp.bfloat16)
    )
    partial_commands = jnp.dot(
        lax.all_gather(slope_vector, "wide", axis=0, tiled=True),
        recon,
        preferred_element_type=jnp.float32,
    )
    partial_commands = partial_commands.reshape(narrow_count, -1, partial_commands.shape[1])
    commands = jnp.sum(lax.all_to_all(partial_commands, "narrow", 0, 0), axis=0)
    return (slopes, commands)


def solution(mesh):
    return jax.shard_map(
        body,
        mesh=mesh,
        in_specs=(P(None, "wide", None), P(), P(None, "narrow", None), P("narrow", "wide")),
        out_specs=(P(None, "wide", None, "narrow", None), P("narrow", "wide")),
        check_vma=False,
    )
```

profile of v0, /device:TPU:1, one launch (start us, length us, event | category | flops | bytes accessed | tf_op | source)
XLA Modules:
  0.0 316.4 jit_solution(13882446086356264635)
XLA Ops:
  13.8 5.6 %fusion.50 = (bf16[1,256,4096]{2,1,0:T(8,128)(2,1)S(1)}, bf16[1,256,4096]{2,1,0:T(8,128)(2,1)}, bf16[1,256,4096]{2,1,0:T(8,128)(2,1)}, bf16[1,256,4096]{2,1,0:T(8,128)(2,1)}) fusion(bf16[4,256,4096]{2,1,0:T(8,128)(2,1)} %param.6), kind=kLoop, calls=%fused_computation.106 | loop fusion | bytes 16777216 | tf_op jit(solution)/shard_map/slice | solution.py:81
  24.4 2.3 dynamic-slice_bitcast_fusion
  26.7 2.0 dynamic-slice_bitcast_fusion.2
  28.8 3.2 %fusion.35 = (bf16[1,144,1344]{2,1,0:T(8,128)(2,1)S(1)}, bf16[1,144,1344]{2,1,0:T(8,128)(2,1)S(1)}, bf16[1,144,1344]{2,1,0:T(8,128)(2,1)S(1)}, bf16[1,144,1344]{2,1,0:T(8,128)(2,1)S(1)}) fusion(s32[]{:T(128)S(6)} %min.13, bf16[144,1344]{1,0:T(8,128)(2,1)S(1)} %broadcast_in_dim.6, bf16[256,1344]{1,0:T(8,128)(2,1)S(1)} %get-tuple-element.220, s32[]{:T(128)S(6)} %min.15, ...), kind=kLoop, calls=%fused_computation.80 | loop fusion | flops 4644864 | bytes 4687888 | tf_op jit(solution)/shard_map/stack | solution.py:88
  32.0 1.4 pad_maximum_fusion
  155.5 4.3 %fusion.48 = bf16[256,1024]{1,0:T(8,128)(2,1)S(1)} fusion(s32[1024]{0:T(1024)S(1)} %get-tuple-element.214, s32[256]{0:T(256)S(1)} %get-tuple-element.215, s32[1024]{0:T(1024)S(1)} %get-tuple-element.213, s32[256]{0:T(256)S(1)} %get-tuple-element.216), kind=kLoop, calls=%fused_computation.104 | loop fusion | flops 5242880 | bytes 534528 | tf_op jit(solution)/shard_map/neg | solution.py:36
  159.9 4.8 %sine_convert_fusion.2 = (bf16[256,1024]{1,0:T(8,128)(2,1)S(1)}, bf16[256,1024]{1,0:T(8,128)(2,1)S(1)}) fusion(s32[1024]{0:T(1024)S(1)} %get-tuple-element.214, s32[256]{0:T(256)S(1)} %get-tuple-element.215, s32[1024]{0:T(1024)S(1)} %get-tuple-element.213, s32[256]{0:T(256)S(1)} %get-tuple-element.216), kind=kLoop, calls=%fused_computation.55 | loop fusion | flops 4718592 | bytes 1058816 | tf_op jit(solution)/shard_map/convert_element_type | solution.py:34
  164.6 1.6 maximum_maximum_fusion
  166.2 1.5 fusion.51
  171.4 1.7 copy-done.1
  173.1 98.5 %while.13 = (s32[]{:T(128)}, f32[4,800,2]{1,2,0:T(2,128)S(1)}, f32[4,2,80,1280]{3,2,1,0:T(8,128)}, bf16[512,2048]{1,0:T(8,128)(2,1)}, f32[800,1]{0,1:T(1,128)S(1)}, /*index=5*/s32[]{:T(128)}, s32[]{:T(128)}, s32[]{}, f32[]{:T(128)}) while((s32[]{:T(128)}, f32[4,800,2]{1,2,0:T(2,128)S(1)}, f32[4,2,80,1280]{3,2,1,0:T(8,128)}, ...), condition=%wide.region_6.7_spmd, body=%wide.region_2.6_spmd.sunk | while | flops 1687980416 | bytes 22656888 | solution.py:117
  173.1 5.2 %cosine_convert_fusion.4 = (bf16[1,1,80,1280]{3,2,1,0:T(8,128)(2,1)}, bf16[1,1,80,1280]{3,2,1,0:T(8,128)(2,1)}, bf16[1,1,80,1280]{3,2,1,0:T(8,128)(2,1)S(1)}, bf16[1,1,80,1280]{3,2,1,0:T(8,128)(2,1)S(1)}) fusion(f32[4,2,80,1280]{3,2,1,0:T(8,128)} %get-tuple-element.294, s32[]{:T(128)} %get-tuple-element.283, s32[]{:T(128)S(6)} %add.637), kind=kLoop, calls=%fused_computation.16.clone.1 | loop fusion | flops 409600 | bytes 1638408 | tf_op jit(solution)/shard_map/convert.15
  178.3 1.2 cos.47
  181.6 2.2 cos.49
  185.8 2.2 sin.47
  192.7 3.8 %fusion.70 = f32[800,2048]{1,0:T(8,128)S(1)} fusion(bf16[512,2048]{1,0:T(8,128)(2,1)} %get-tuple-element.295, bf16[400,256]{0,1:T(8,128)(2,1)} %sin.48, bf16[400,256]{0,1:T(8,128)(2,1)} %cos.48, bf16[400,256]{0,1:T(8,128)(2,1)S(1)} %sin.50, bf16[400,256]{0,1:T(8,128)(2,1)} %cos.50), kind=kOutput, calls=%fused_computation.5.clone.1 | convolution fusion | flops 1680998400 | bytes 9469952 | tf_op jit(solution)/shard_map/while/body/eval_jaxpr/dot_general | solution.py:52
  197.7 5.2 %cosine_convert_fusion.4 = (bf16[1,1,80,1280]{3,2,1,0:T(8,128)(2,1)}, bf16[1,1,80,1280]{3,2,1,0:T(8,128)(2,1)}, bf16[1,1,80,1280]{3,2,1,0:T(8,128)(2,1)S(1)}, bf16[1,1,80,1280]{3,2,1,0:T(8,128)(2,1)S(1)}) fusion(f32[4,2,80,1280]{3,2,1,0:T(8,128)} %get-tuple-element.294, s32[]{:T(128)} %get-tuple-element.283, s32[]{:T(128)S(6)} %add.637), kind=kLoop, calls=%fused_computation.16.clone.1 | loop fusion | flops 409600 | bytes 1638408 | tf_op jit(solution)/shard_map/convert.15
  202.9 1.2 cos.47
  206.2 2.2 cos.49
  210.5 2.2 sin.47
  217.3 3.9 %fusion.70 = f32[800,2048]{1,0:T(8,128)S(1)} fusion(bf16[512,2048]{1,0:T(8,128)(2,1)} %get-tuple-element.295, bf16[400,256]{0,1:T(8,128)(2,1)} %sin.48, bf16[400,256]{0,1:T(8,128)(2,1)} %cos.48, bf16[400,256]{0,1:T(8,128)(2,1)S(1)} %sin.50, bf16[400,256]{0,1:T(8,128)(2,1)} %cos.50), kind=kOutput, calls=%fused_computation.5.clone.1 | convolution fusion | flops 1680998400 | bytes 9469952 | tf_op jit(solution)/shard_map/while/body/eval_jaxpr/dot_general | solution.py:52
  222.4 5.2 %cosine_convert_fusion.4 = (bf16[1,1,80,1280]{3,2,1,0:T(8,128)(2,1)}, bf16[1,1,80,1280]{3,2,1,0:T(8,128)(2,1)}, bf16[1,1,80,1280]{3,2,1,0:T(8,128)(2,1)S(1)}, bf16[1,1,80,1280]{3,2,1,0:T(8,128)(2,1)S(1)}) fusion(f32[4,2,80,1280]{3,2,1,0:T(8,128)} %get-tuple-element.294, s32[]{:T(128)} %get-tuple-element.283, s32[]{:T(128)S(6)} %add.637), kind=kLoop, calls=%fused_computation.16.clone.1 | loop fusion | flops 409600 | bytes 1638408 | tf_op jit(solution)/shard_map/convert.15
  230.8 2.2 cos.49
  235.1 2.2 sin.47
  241.9 3.9 %fusion.70 = f32[800,2048]{1,0:T(8,128)S(1)} fusion(bf16[512,2048]{1,0:T(8,128)(2,1)} %get-tuple-element.295, bf16[400,256]{0,1:T(8,128)(2,1)} %sin.48, bf16[400,256]{0,1:T(8,128)(2,1)} %cos.48, bf16[400,256]{0,1:T(8,128)(2,1)S(1)} %sin.50, bf16[400,256]{0,1:T(8,128)(2,1)} %cos.50), kind=kOutput, calls=%fused_computation.5.clone.1 | convolution fusion | flops 1680998400 | bytes 9469952 | tf_op jit(solution)/shard_map/while/body/eval_jaxpr/dot_general | solution.py:52
  247.0 5.2 %cosine_convert_fusion.4 = (bf16[1,1,80,1280]{3,2,1,0:T(8,128)(2,1)}, bf16[1,1,80,1280]{3,2,1,0:T(8,128)(2,1)}, bf16[1,1,80,1280]{3,2,1,0:T(8,128)(2,1)S(1)}, bf16[1,1,80,1280]{3,2,1,0:T(8,128)(2,1)S(1)}) fusion(f32[4,2,80,1280]{3,2,1,0:T(8,128)} %get-tuple-element.294, s32[]{:T(128)} %get-tuple-element.283, s32[]{:T(128)S(6)} %add.637), kind=kLoop, calls=%fused_computation.16.clone.1 | loop fusion | flops 409600 | bytes 1638408 | tf_op jit(solution)/shard_map/convert.15
  255.5 2.2 cos.49
  259.7 2.2 sin.47
  266.6 3.8 %fusion.70 = f32[800,2048]{1,0:T(8,128)S(1)} fusion(bf16[512,2048]{1,0:T(8,128)(2,1)} %get-tuple-element.295, bf16[400,256]{0,1:T(8,128)(2,1)} %sin.48, bf16[400,256]{0,1:T(8,128)(2,1)} %cos.48, bf16[400,256]{0,1:T(8,128)(2,1)S(1)} %sin.50, bf16[400,256]{0,1:T(8,128)(2,1)} %cos.50), kind=kOutput, calls=%fused_computation.5.clone.1 | convolution fusion | flops 1680998400 | bytes 9469952 | tf_op jit(solution)/shard_map/while/body/eval_jaxpr/dot_general | solution.py:52
  272.3 21.9 %all-gather = bf16[16,4,1600]{2,1,0:T(4,128)(2,1)S(1)} all-gather(bf16[1,4,1600]{2,1,0:T(4,128)(2,1)S(1)} %copy.28), channel_id=1, replica_groups=mesh['wide'=16,'narrow'=16] {'wide'}, dimensions={0}, use_global_device_ids=true | all-gather | bytes 217600 | tf_op jit(solution)/shard_map/all_gather | solution.py:126
  295.5 6.8 %all-to-all-start = ((f32[16,4,320]{2,1,0:T(4,128)}), f32[16,4,320]{2,1,0:T(4,128)S(1)}, u32[]{:S(2)}, u32[]{:S(2)}) async-start(f32[16,4,320]{2,1,0:T(4,128)} %reshape.294), calls=%async_computation | async-start | bytes 196608 | tf_op jit(solution)/shard_map/all_to_all | solution.py:131
  302.9 6.0 %all-to-all-done = f32[16,4,320]{2,1,0:T(4,128)S(1)} async-done(((f32[16,4,320]{2,1,0:T(4,128)}), f32[16,4,320]{2,1,0:T(4,128)S(1)}, u32[]{:S(2)}, u32[]{:S(2)}) %all-to-all-start) | async-done | bytes 81952 | tf_op jit(solution)/shard_map/all_to_all | solution.py:131
  (107 shorter events, 53.2 us)
Async XLA Ops:
  7.2 287.2 %copy-start = (bf16[1600,320]{0,1:T(8,128)(2,1)S(1)}, bf16[1600,320]{0,1:T(8,128)(2,1)}, u32[]{:S(2)}) copy-start(bf16[1600,320]{0,1:T(8,128)(2,1)} %param.9) | copy-start | bytes 3072004
  7.2 159.0 %all-reduce.2.cloned.1.call-start = ((), (), s32[]{:S(2)}) async-start(), calls=%async_computation.1 | async-start | bytes 3244032 | tf_op jit(solution)/shard_map/psum | solution.py:88
  32.0 1.5 copy-start.2
  32.0 83.7 %copy-start.3 = (s32[2,5,80]{2,0,1:T(2,128)S(1)}, s32[2,5,80]{2,0,1:T(2,128)}, u32[]{:S(2)}) copy-start(s32[2,5,80]{2,0,1:T(2,128)} %param.8) | copy-start | bytes 9604
  171.4 1.7 copy-start.1
  295.5 13.5 %all-to-all-start = ((f32[16,4,320]{2,1,0:T(4,128)}), f32[16,4,320]{2,1,0:T(4,128)S(1)}, u32[]{:S(2)}, u32[]{:S(2)}) async-start(f32[16,4,320]{2,1,0:T(4,128)} %reshape.294), calls=%async_computation | async-start | bytes 196608 | tf_op jit(solution)/shard_map/all_to_all | solution.py:131
Sparse Core Ops, SparseCore 0:
  33.6 116.6 all-reduce.1
where the time goes:
time: 320 us; the launch traced here: 316 us
  between operations  143 us (45%)
  local copies, waits for them, and re-layouts  76 us (24%)
  other arithmetic  46 us (14%)
  blocking collectives  21.9 us (7%)
  matrix products  15.8 us (5%)
  starting transfers between devices  6.82 us (2%)
  waiting for transfers between devices  6.04 us (2%)
    cos x24, local copies, waits for them, and re-layouts, subaperture_fields(): jnp.cos(samples)  30.1 us
    sin x24, local copies, waits for them, and re-layouts, subaperture_fields(): jnp.sin(samples)  27.1 us
    all_gather x1, blocking collectives, body(): lax.all_gather(slope_vector, 'wide', axis=0, tiled=True)  21.9 us
    another operation x8, other arithmetic  20.9 us
    dot_general x4, matrix products, centroids(): spectrum = jnp.dot(fields, transform, preferred_element_type=jnp.float32)  15.4 us
    all_to_all x1, starting transfers between devices, body(): commands = jnp.sum(lax.all_to_all(partial_commands, 'narrow', 0, 0), axis=0)  6.79 us
  transfers between devices with their start and end apart: 2, of which 1 were waited for; matrix products, arithmetic and copies ran while one was open for 5% of the time, Pallas kernels for 0%

commit v1 on v0

--- a/solution.py
+++ b/solution.py
@@ -123,7 +123,9 @@
         .astype(jnp.bfloat16)
     )
     partial_commands = jnp.dot(
-        lax.all_gather(slope_vector, "wide", axis=0, tiled=True),
+        jnp.concatenate(
+            lax.all_to_all(jnp.stack([slope_vector] * lax.axis_size("wide")), "wide", 0, 0), axis=0
+        ),
         recon,
         preferred_element_type=jnp.float32,
     )

time: 320 us -> 319 us (level)
    all_gather x1 -> x0, blocking collectives: 21.9 us -> none  [body(): lax.all_gather(slope_vector, 'wide', axis=0, tiled=True)]
    all_to_all x0 -> x1, blocking collectives: none -> 20.5 us  [body(): lax.all_to_all(jnp.stack([slope_vector] * lax.axis_size('wide')), 'wide',...]
where the time goes in v1:
time: 319 us; the launch traced here: 315 us
  between operations  143 us (45%)
  local copies, waits for them, and re-layouts  76 us (24%)
  other arithmetic  46 us (14%)
  blocking collectives  20.5 us (6%)
  matrix products  15.8 us (5%)
  starting transfers between devices  6.78 us (2%)
  waiting for transfers between devices  6.52 us (2%)
    cos x24, local copies, waits for them, and re-layouts, subaperture_fields(): jnp.cos(samples)  30.1 us
    sin x24, local copies, waits for them, and re-layouts, subaperture_fields(): jnp.sin(samples)  27.1 us
    another operation x8, other arithmetic  20.9 us
    all_to_all x1, blocking collectives, body(): lax.all_to_all(jnp.stack([slope_vector] * lax.axis_size('wide')), 'wide',...  20.5 us
    dot_general x4, matrix products, centroids(): spectrum = jnp.dot(fields, transform, preferred_element_type=jnp.float32)  15.4 us
    all_to_all x1, starting transfers between devices, body(): commands = jnp.sum(lax.all_to_all(partial_commands, 'narrow', 0, 0), axis=0)  6.74 us
    all_to_all x1, waiting for transfers between devices, body(): commands = jnp.sum(lax.all_to_all(partial_commands, 'narrow', 0, 0), axis=0)  6.51 us
  transfers between devices with their start and end apart: 2, of which 1 were waited for; matrix products, arithmetic and copies ran while one was open for 5% of the time, Pallas kernels for 0%

profile of v1, /device:TPU:1, one launch (start us, length us, event | category | flops | bytes accessed | tf_op | source)
XLA Modules:
  0.0 315.4 jit_solution(17006792417511825724)
XLA Ops:
  13.8 5.6 %fusion.53 = (bf16[1,256,4096]{2,1,0:T(8,128)(2,1)S(1)}, bf16[1,256,4096]{2,1,0:T(8,128)(2,1)}, bf16[1,256,4096]{2,1,0:T(8,128)(2,1)}, bf16[1,256,4096]{2,1,0:T(8,128)(2,1)}) fusion(bf16[4,256,4096]{2,1,0:T(8,128)(2,1)} %param.6), kind=kLoop, calls=%fused_computation.109 | loop fusion | bytes 16777216 | tf_op jit(solution)/shard_map/slice | solution.py:81
  24.4 2.3 dynamic-slice_bitcast_fusion
  26.7 2.0 dynamic-slice_bitcast_fusion.2
  28.8 3.2 %fusion.37 = (bf16[1,144,1344]{2,1,0:T(8,128)(2,1)S(1)}, bf16[1,144,1344]{2,1,0:T(8,128)(2,1)S(1)}, bf16[1,144,1344]{2,1,0:T(8,128)(2,1)S(1)}, bf16[1,144,1344]{2,1,0:T(8,128)(2,1)S(1)}) fusion(s32[]{:T(128)S(6)} %min.13, bf16[144,1344]{1,0:T(8,128)(2,1)S(1)} %broadcast_in_dim.6, bf16[256,1344]{1,0:T(8,128)(2,1)S(1)} %get-tuple-element.218, s32[]{:T(128)S(6)} %min.15, ...), kind=kLoop, calls=%fused_computation.82 | loop fusion | flops 4644864 | bytes 4687888 | tf_op jit(solution)/shard_map/stack | solution.py:88
  32.0 1.4 pad_maximum_fusion
  155.5 4.3 %fusion.51 = bf16[256,1024]{1,0:T(8,128)(2,1)S(1)} fusion(s32[1024]{0:T(1024)S(1)} %get-tuple-element.212, s32[256]{0:T(256)S(1)} %get-tuple-element.213, s32[1024]{0:T(1024)S(1)} %get-tuple-element.211, s32[256]{0:T(256)S(1)} %get-tuple-element.214), kind=kLoop, calls=%fused_computation.107 | loop fusion | flops 5242880 | bytes 534528 | tf_op jit(solution)/shard_map/neg | solution.py:36
  159.9 4.8 %sine_convert_fusion.2 = (bf16[256,1024]{1,0:T(8,128)(2,1)S(1)}, bf16[256,1024]{1,0:T(8,128)(2,1)S(1)}) fusion(s32[1024]{0:T(1024)S(1)} %get-tuple-element.212, s32[256]{0:T(256)S(1)} %get-tuple-element.213, s32[1024]{0:T(1024)S(1)} %get-tuple-element.211, s32[256]{0:T(256)S(1)} %get-tuple-element.214), kind=kLoop, calls=%fused_computation.57 | loop fusion | flops 4718592 | bytes 1058816 | tf_op jit(solution)/shard_map/convert_element_type | solution.py:34
  164.6 1.6 maximum_maximum_fusion
  166.2 1.5 fusion.54
  171.4 1.7 copy-done.1
  173.1 98.5 %while.13 = (s32[]{:T(128)}, f32[4,800,2]{1,2,0:T(2,128)S(1)}, f32[4,2,80,1280]{3,2,1,0:T(8,128)}, bf16[512,2048]{1,0:T(8,128)(2,1)}, f32[800,1]{0,1:T(1,128)S(1)}, /*index=5*/s32[]{:T(128)}, s32[]{:T(128)}, s32[]{}, f32[]{:T(128)}) while((s32[]{:T(128)}, f32[4,800,2]{1,2,0:T(2,128)S(1)}, f32[4,2,80,1280]{3,2,1,0:T(8,128)}, ...), condition=%wide.region_6.7_spmd, body=%wide.region_2.6_spmd.sunk | while | flops 1687980416 | bytes 22656888 | solution.py:117
  173.1 5.2 %cosine_convert_fusion.4 = (bf16[1,1,80,1280]{3,2,1,0:T(8,128)(2,1)}, bf16[1,1,80,1280]{3,2,1,0:T(8,128)(2,1)}, bf16[1,1,80,1280]{3,2,1,0:T(8,128)(2,1)S(1)}, bf16[1,1,80,1280]{3,2,1,0:T(8,128)(2,1)S(1)}) fusion(f32[4,2,80,1280]{3,2,1,0:T(8,128)} %get-tuple-element.292, s32[]{:T(128)} %get-tuple-element.281, s32[]{:T(128)S(6)} %add.637), kind=kLoop, calls=%fused_computation.16.clone.1 | loop fusion | flops 409600 | bytes 1638408 | tf_op jit(solution)/shard_map/convert.15
  178.3 1.2 cos.47
  181.6 2.2 cos.49
  185.8 2.2 sin.47
  192.7 3.8 %fusion.70 = f32[800,2048]{1,0:T(8,128)S(1)} fusion(bf16[512,2048]{1,0:T(8,128)(2,1)} %get-tuple-element.293, bf16[400,256]{0,1:T(8,128)(2,1)} %sin.48, bf16[400,256]{0,1:T(8,128)(2,1)} %cos.48, bf16[400,256]{0,1:T(8,128)(2,1)S(1)} %sin.50, bf16[400,256]{0,1:T(8,128)(2,1)} %cos.50), kind=kOutput, calls=%fused_computation.5.clone.1 | convolution fusion | flops 1680998400 | bytes 9469952 | tf_op jit(solution)/shard_map/while/body/eval_jaxpr/dot_general | solution.py:52
  197.7 5.2 %cosine_convert_fusion.4 = (bf16[1,1,80,1280]{3,2,1,0:T(8,128)(2,1)}, bf16[1,1,80,1280]{3,2,1,0:T(8,128)(2,1)}, bf16[1,1,80,1280]{3,2,1,0:T(8,128)(2,1)S(1)}, bf16[1,1,80,1280]{3,2,1,0:T(8,128)(2,1)S(1)}) fusion(f32[4,2,80,1280]{3,2,1,0:T(8,128)} %get-tuple-element.292, s32[]{:T(128)} %get-tuple-element.281, s32[]{:T(128)S(6)} %add.637), kind=kLoop, calls=%fused_computation.16.clone.1 | loop fusion | flops 409600 | bytes 1638408 | tf_op jit(solution)/shard_map/convert.15
  202.9 1.2 cos.47
  206.2 2.2 cos.49
  210.5 2.2 sin.47
  217.3 3.9 %fusion.70 = f32[800,2048]{1,0:T(8,128)S(1)} fusion(bf16[512,2048]{1,0:T(8,128)(2,1)} %get-tuple-element.293, bf16[400,256]{0,1:T(8,128)(2,1)} %sin.48, bf16[400,256]{0,1:T(8,128)(2,1)} %cos.48, bf16[400,256]{0,1:T(8,128)(2,1)S(1)} %sin.50, bf16[400,256]{0,1:T(8,128)(2,1)} %cos.50), kind=kOutput, calls=%fused_computation.5.clone.1 | convolution fusion | flops 1680998400 | bytes 9469952 | tf_op jit(solution)/shard_map/while/body/eval_jaxpr/dot_general | solution.py:52
  222.4 5.2 %cosine_convert_fusion.4 = (bf16[1,1,80,1280]{3,2,1,0:T(8,128)(2,1)}, bf16[1,1,80,1280]{3,2,1,0:T(8,128)(2,1)}, bf16[1,1,80,1280]{3,2,1,0:T(8,128)(2,1)S(1)}, bf16[1,1,80,1280]{3,2,1,0:T(8,128)(2,1)S(1)}) fusion(f32[4,2,80,1280]{3,2,1,0:T(8,128)} %get-tuple-element.292, s32[]{:T(128)} %get-tuple-element.281, s32[]{:T(128)S(6)} %add.637), kind=kLoop, calls=%fused_computation.16.clone.1 | loop fusion | flops 409600 | bytes 1638408 | tf_op jit(solution)/shard_map/convert.15
  230.8 2.2 cos.49
  235.1 2.2 sin.47
  241.9 3.9 %fusion.70 = f32[800,2048]{1,0:T(8,128)S(1)} fusion(bf16[512,2048]{1,0:T(8,128)(2,1)} %get-tuple-element.293, bf16[400,256]{0,1:T(8,128)(2,1)} %sin.48, bf16[400,256]{0,1:T(8,128)(2,1)} %cos.48, bf16[400,256]{0,1:T(8,128)(2,1)S(1)} %sin.50, bf16[400,256]{0,1:T(8,128)(2,1)} %cos.50), kind=kOutput, calls=%fused_computation.5.clone.1 | convolution fusion | flops 1680998400 | bytes 9469952 | tf_op jit(solution)/shard_map/while/body/eval_jaxpr/dot_general | solution.py:52
  247.0 5.2 %cosine_convert_fusion.4 = (bf16[1,1,80,1280]{3,2,1,0:T(8,128)(2,1)}, bf16[1,1,80,1280]{3,2,1,0:T(8,128)(2,1)}, bf16[1,1,80,1280]{3,2,1,0:T(8,128)(2,1)S(1)}, bf16[1,1,80,1280]{3,2,1,0:T(8,128)(2,1)S(1)}) fusion(f32[4,2,80,1280]{3,2,1,0:T(8,128)} %get-tuple-element.292, s32[]{:T(128)} %get-tuple-element.281, s32[]{:T(128)S(6)} %add.637), kind=kLoop, calls=%fused_computation.16.clone.1 | loop fusion | flops 409600 | bytes 1638408 | tf_op jit(solution)/shard_map/convert.15
  255.5 2.2 cos.49
  259.7 2.2 sin.47
  266.6 3.8 %fusion.70 = f32[800,2048]{1,0:T(8,128)S(1)} fusion(bf16[512,2048]{1,0:T(8,128)(2,1)} %get-tuple-element.293, bf16[400,256]{0,1:T(8,128)(2,1)} %sin.48, bf16[400,256]{0,1:T(8,128)(2,1)} %cos.48, bf16[400,256]{0,1:T(8,128)(2,1)S(1)} %sin.50, bf16[400,256]{0,1:T(8,128)(2,1)} %cos.50), kind=kOutput, calls=%fused_computation.5.clone.1 | convolution fusion | flops 1680998400 | bytes 9469952 | tf_op jit(solution)/shard_map/while/body/eval_jaxpr/dot_general | solution.py:52
  272.4 20.5 %all_to_all.10 = bf16[16,4,1600]{2,1,0:T(4,128)(2,1)S(1)} all-to-all(bf16[16,4,1600]{2,1,0:T(4,128)(2,1)S(1)} %stack.29), channel_id=1, replica_groups=mesh['wide'=16,'narrow'=16] {'wide'}, dimensions={0} | all-to-all | bytes 409600 | tf_op jit(solution)/shard_map/all_to_all | solution.py:127
  294.0 6.7 %all-to-all-start.1 = ((f32[16,4,320]{2,1,0:T(4,128)}), f32[16,4,320]{2,1,0:T(4,128)S(1)}, u32[]{:S(2)}, u32[]{:S(2)}) async-start(f32[16,4,320]{2,1,0:T(4,128)} %copy.23), calls=%async_computation.1 | async-start | bytes 196608 | tf_op jit(solution)/shard_map/all_to_all | solution.py:133
  301.4 6.5 %all-to-all-done.1 = f32[16,4,320]{2,1,0:T(4,128)S(1)} async-done(((f32[16,4,320]{2,1,0:T(4,128)}), f32[16,4,320]{2,1,0:T(4,128)S(1)}, u32[]{:S(2)}, u32[]{:S(2)}) %all-to-all-start.1) | async-done | bytes 81952 | tf_op jit(solution)/shard_map/all_to_all | solution.py:133
  (107 shorter events, 53.1 us)
Async XLA Ops:
  7.2 285.8 %copy-start = (bf16[1600,320]{0,1:T(8,128)(2,1)S(1)}, bf16[1600,320]{0,1:T(8,128)(2,1)}, u32[]{:S(2)}) copy-start(bf16[1600,320]{0,1:T(8,128)(2,1)} %param.9) | copy-start | bytes 3072004
  7.2 159.0 %all-reduce.2.cloned.1.call-start = ((), (), s32[]{:S(2)}) async-start(), calls=%async_computation.2 | async-start | bytes 3244032 | tf_op jit(solution)/shard_map/psum | solution.py:88
  32.0 1.5 copy-start.2
  32.0 83.7 %copy-start.3 = (s32[2,5,80]{2,0,1:T(2,128)S(1)}, s32[2,5,80]{2,0,1:T(2,128)}, u32[]{:S(2)}) copy-start(s32[2,5,80]{2,0,1:T(2,128)} %param.8) | copy-start | bytes 9604
  171.4 1.7 copy-start.1
  294.0 13.9 %all-to-all-start.1 = ((f32[16,4,320]{2,1,0:T(4,128)}), f32[16,4,320]{2,1,0:T(4,128)S(1)}, u32[]{:S(2)}, u32[]{:S(2)}) async-start(f32[16,4,320]{2,1,0:T(4,128)} %copy.23), calls=%async_computation.1 | async-start | bytes 196608 | tf_op jit(solution)/shard_map/all_to_all | solution.py:133
Sparse Core Ops, SparseCore 0:
  33.6 116.6 all-reduce.1
